TPU v7x, 256 devices: a whole 4x4x8 slice. The times are simulated.
256 devices in a mesh: kv: 8 (over z), blk: 32 (over y, x, core).
Axes of the slice: x: 4, y: 4, z: 8, core: 2. Of those that a mesh axis runs over, the one named last changes fastest.
Arguments:
- embeds: bfloat16 [1, 256, 3072], P(None, None, 'blk'), may hold values from -40 to 40
- attn_norm: float32 [3072], P('blk'), may hold values from 0.25 to 1.75
- query_key_value_weight: bfloat16 [3072, 5120], P('blk', 'kv'), may hold values from -0.109375 to 0.109375
- w_out: bfloat16 [3072, 3072], P('kv', 'blk'), may hold values from -0.109375 to 0.109375
- mlp_norm: float32 [3072], P('blk'), may hold values from 0.25 to 1.75
- w_gate: bfloat16 [3072, 8192], P('blk', 'kv'), may hold values from -0.109375 to 0.109375
- w_up: bfloat16 [3072, 8192], P('blk', 'kv'), may hold values from -0.109375 to 0.109375
- w_down: bfloat16 [8192, 3072], P('kv', 'blk'), may hold values from -0.0625 to 0.0625
- prompt_key_slots: bfloat16 [256, 8, 128, 128], P('blk', 'kv'), may hold values from -210 to 210
- prompt_value_slots: bfloat16 [256, 8, 128, 128], P('blk', 'kv'), may hold values from -6 to 6
- generated_keys: bfloat16 [256, 8, 127, 128], P('blk', 'kv'), may hold values from -10 to 10
- generated_values: bfloat16 [256, 8, 127, 128], P('blk', 'kv'), may hold values from -6 to 6
- parents: int32 [1, 256], P(None, 'blk'), may hold values from 0 to 7
- prompt_length: int32 [32], replicated, may hold values from 1024 to 8192
- tenant_bounds: int32 [5], replicated, may hold values from 0 to 32, as said below
- slot_table: int32 [256], P('blk'), may hold values from 0 to 256, as said below
Outputs:
- hidden_out: float32 [1, 256, 3072], P(None, None, 'blk')
- keys_out: bfloat16 [256, 8, 128, 128], P('blk', 'kv')
- values_out: bfloat16 [256, 8, 128, 128], P('blk', 'kv')
Inputs may be any that keep to these rules, and one draw needn't show every extreme that they name: parents[s, b] is the beam, among the 8 beams of b's request, whose cache beam b continues at step s. tenant_bounds[0] = 0 and tenant_bounds[4] = 32, strictly rising. `slot_table`: with L_t the largest prompt_length of tenant t's requests, every block j below ceil(L_t / 128) of every tenant t stands in exactly one slot as t * 64 + j, no other block stands anywhere, and 256 marks an empty slot.
All inputs are finite; a program needn't handle non-finite values.
Results may differ from a plain program's by a relative error of at most 0.012.
The roundings to bfloat16 on the way count: a program that leaves them out, or rounds other values in their place, can miss the bound.
Values may be sent and summed in bfloat16 or wider, within the bound.
No kernel may reach another device: no remote copies, remote signals or barrier semaphores. Data moves between devices by JAX's collectives and lax.ppermute only.
A program may use at most 64 MiB of HBM per device.

v0:
```python
import math
import jax
import jax.numpy as jnp
from jax import lax
from jax.sharding import PartitionSpec as P

MODEL_WIDTH = 3072
QUERY_HEADS = 24
KEY_VALUE_HEADS = 8
HEAD_WIDTH = 128
REQUEST_BEAMS = 8
TENANT_COUNT = 4
BLOCK_POSITIONS = 128
PROMPT_BLOCKS = 64
EARLIER_TOKENS = 127
DECODE_STEPS = 1
masked_score = -1e30


def exchange(value, axis, bit):
    count = lax.axis_size(axis)
    return lax.ppermute(value, axis, [(i, i ^ 1 << bit) for i in range(count)])


def butterfly_sum(value, axis):
    count = lax.axis_size(axis)
    if count & count - 1:
        return lax.psum(value, axis)
    for bit in range(count.bit_length() - 1):
        value = value + exchange(value, axis, bit)
    return value


def scatter_sum(value, axis):
    count = lax.axis_size(axis)
    pieces = value.reshape((count, value.shape[0] // count) + value.shape[1:])
    return jnp.sum(lax.all_to_all(pieces, axis, 0, 0, tiled=False), axis=0)


def rotate(values, angles):
    half = values.shape[-1] // 2
    first = values[..., :half]
    second = values[..., half:]
    cosine = jnp.cos(angles)
    sine = jnp.sin(angles)
    return jnp.concatenate(
        [first * cosine - second * sine, second * cosine + first * sine], axis=-1
    )


def angles_for(positions, head_size):
    half = head_size // 2
    freq = jnp.exp(jnp.arange(half, dtype=jnp.float32) * (-math.log(500000.0) / half))
    return positions.astype(jnp.float32)[:, None] * freq[None, :]


def across_heads(partial_value):
    return butterfly_sum(partial_value, "kv")


def body(
    embeds,
    attn_norm,
    query_key_value_weight,
    w_out,
    mlp_norm,
    w_gate,
    w_up,
    w_down,
    prompt_key_slots,
    prompt_value_slots,
    generated_keys,
    generated_values,
    parents,
    prompt_length,
    tenant_bounds,
    slot_table,
):
    blocks = lax.axis_size("blk")
    my_index = lax.axis_index("blk")
    all_rows = embeds.shape[1]
    own_rows = all_rows // blocks
    heads_kv = prompt_key_slots.shape[1]
    slots_here = prompt_key_slots.shape[0]
    keys_here = slots_here * BLOCK_POSITIONS
    group_queries = QUERY_HEADS // KEY_VALUE_HEADS
    col_width = group_queries + 2
    score_scale = 1.0 / math.sqrt(HEAD_WIDTH)
    unit_count = w_gate.shape[1]
    beam_req = jnp.arange(all_rows, dtype=jnp.int32) // REQUEST_BEAMS
    tenant_beam = jnp.sum(
        (beam_req[:, None] >= tenant_bounds[None, 1:TENANT_COUNT]).astype(jnp.int32), axis=1
    )
    length_beam = jnp.repeat(prompt_length, REQUEST_BEAMS)
    slot_tenant = jnp.repeat(slot_table // PROMPT_BLOCKS, BLOCK_POSITIONS)
    slot_pos = jnp.repeat(slot_table % PROMPT_BLOCKS * BLOCK_POSITIONS, BLOCK_POSITIONS) + jnp.tile(
        jnp.arange(BLOCK_POSITIONS, dtype=jnp.int32), slots_here
    )
    visible = (tenant_beam[:, None] == slot_tenant[None, :]) & (
        slot_pos[None, :] < length_beam[:, None]
    )
    prompt_mask = visible[None, :, None, :]
    keys_flat = prompt_key_slots.transpose(1, 0, 2, 3).reshape(heads_kv, keys_here, HEAD_WIDTH)
    values_flat = prompt_value_slots.transpose(1, 0, 2, 3).reshape(heads_kv, keys_here, HEAD_WIDTH)
    local_beam = jnp.arange(own_rows, dtype=jnp.int32)
    base_rows = local_beam // REQUEST_BEAMS * REQUEST_BEAMS
    trailing_zeros = jnp.zeros((own_rows, heads_kv, DECODE_STEPS, HEAD_WIDTH), jnp.bfloat16)
    cached_key_rows = jnp.concatenate([generated_keys, trailing_zeros], axis=2)
    cached_value_rows = jnp.concatenate([generated_values, trailing_zeros], axis=2)
    gen_pos = jnp.arange(EARLIER_TOKENS + DECODE_STEPS, dtype=jnp.int32)
    w_both = jnp.concatenate([w_gate, w_up], axis=1)
    residual = embeds[0].astype(jnp.float32)
    squares = jnp.sum(residual * residual, axis=1)
    normed = (residual * attn_norm).astype(jnp.bfloat16)
    partial_value = jnp.dot(normed, query_key_value_weight, preferred_element_type=jnp.float32)
    own_value = scatter_sum(jnp.concatenate([partial_value, squares[:, None]], axis=1), "blk")
    inverse = lax.rsqrt(own_value[:, -1] / MODEL_WIDTH + 1e-05)
    own_proj = (own_value[:, :-1] * inverse[:, None]).reshape(
        own_rows, heads_kv, col_width, HEAD_WIDTH
    )
    own_length = lax.dynamic_slice_in_dim(length_beam, my_index * own_rows, own_rows, 0)
    own_angle = angles_for(own_length + EARLIER_TOKENS + 0, HEAD_WIDTH)
    own_queries = rotate(own_proj[:, :, :group_queries], own_angle[:, None, None, :]).astype(
        jnp.bfloat16
    )
    query_rows = lax.all_gather(own_queries, "blk", axis=0, tiled=True)
    new_key = rotate(own_proj[:, :, group_queries], own_angle[:, None, :]).astype(jnp.bfloat16)
    new_value = own_proj[:, :, group_queries + 1].astype(jnp.bfloat16)
    parent_rows = base_rows + parents[0]
    cached_key_rows = (
        jnp.take(cached_key_rows, parent_rows, axis=0).at[:, :, EARLIER_TOKENS].set(new_key)
    )
    cached_value_rows = (
        jnp.take(cached_value_rows, parent_rows, axis=0).at[:, :, EARLIER_TOKENS].set(new_value)
    )
    grouped = query_rows.transpose(1, 0, 2, 3).reshape(
        heads_kv, all_rows * group_queries, HEAD_WIDTH
    )
    scores = jnp.einsum("kqd,knd->kqn", grouped, keys_flat, preferred_element_type=jnp.float32)
    scores = scores.reshape(heads_kv, all_rows, group_queries, keys_here) * score_scale
    top_score = jnp.max(jnp.where(prompt_mask, scores, masked_score), axis=3)
    weights = jnp.where(prompt_mask, jnp.exp(scores - top_score[..., None]), 0.0)
    total_mass = jnp.sum(weights, axis=3)
    flat_weights = weights.reshape(heads_kv, all_rows * group_queries, keys_here).astype(
        jnp.bfloat16
    )
    summed = jnp.einsum(
        "kqn,knd->kqd", flat_weights, values_flat, preferred_element_type=jnp.float32
    )
    summed = summed.reshape(heads_kv, all_rows, group_queries, HEAD_WIDTH)
    packed = jnp.concatenate([summed, top_score[..., None], total_mass[..., None]], axis=3)
    packed = packed.transpose(1, 0, 2, 3).reshape(
        blocks, own_rows, heads_kv, group_queries, HEAD_WIDTH + 2
    )
    parts = lax.all_to_all(packed, "blk", 0, 0, tiled=False)
    part_top = parts[..., HEAD_WIDTH]
    prompt_top = jnp.max(part_top, axis=0)
    part_factor = jnp.exp(part_top - prompt_top[None])
    prompt_mass = jnp.sum(parts[..., HEAD_WIDTH + 1] * part_factor, axis=0)
    prompt_sum = jnp.sum(parts[..., :HEAD_WIDTH] * part_factor[..., None], axis=0)
    prompt_top = prompt_top.transpose(1, 0, 2)
    prompt_mass = prompt_mass.transpose(1, 0, 2)
    prompt_sum = prompt_sum.transpose(1, 0, 2, 3)
    gen_scores = (
        jnp.einsum(
            "bkgd,bknd->kbgn", own_queries, cached_key_rows, preferred_element_type=jnp.float32
        )
        * score_scale
    )
    live = (gen_pos <= EARLIER_TOKENS)[None, None, None, :]
    gen_top = jnp.max(jnp.where(live, gen_scores, masked_score), axis=3)
    best = jnp.maximum(prompt_top, gen_top)
    gen_weights = jnp.where(live, jnp.exp(gen_scores - best[..., None]), 0.0)
    shift = jnp.exp(prompt_top - best)
    full_mass = prompt_mass * shift + jnp.sum(gen_weights, axis=3)
    gen_sum = jnp.einsum(
        "kbgn,bknd->kbgd",
        gen_weights.astype(jnp.bfloat16),
        cached_value_rows,
        preferred_element_type=jnp.float32,
    )
    attended_output = (prompt_sum * shift[..., None] + gen_sum) / full_mass[..., None]
    heads_out = (
        attended_output.transpose(1, 0, 2, 3)
        .reshape(own_rows, heads_kv * group_queries * HEAD_WIDTH)
        .astype(jnp.bfloat16)
    )
    head_part = jnp.dot(
        lax.all_gather(heads_out, "blk", axis=0, tiled=True),
        w_out,
        preferred_element_type=jnp.float32,
    )
    after_attn = residual + across_heads(head_part)
    squares2 = jnp.sum(after_attn * after_attn, axis=1)
    normed2 = (after_attn * mlp_norm).astype(jnp.bfloat16)
    mixed = scatter_sum(
        jnp.concatenate(
            [jnp.dot(normed2, w_both, preferred_element_type=jnp.float32), squares2[:, None]],
            axis=1,
        ),
        "blk",
    )
    own_inverse = lax.rsqrt(mixed[:, -1] / MODEL_WIDTH + 1e-05)
    gate = mixed[:, :unit_count] * own_inverse[:, None]
    upper = mixed[:, unit_count : 2 * unit_count] * own_inverse[:, None]
    hidden = (jax.nn.silu(gate) * upper).astype(jnp.bfloat16)
    ff_part = jnp.dot(
        lax.all_gather(hidden, "blk", axis=0, tiled=True),
        w_down,
        preferred_element_type=jnp.float32,
    )
    outputs = [after_attn + across_heads(ff_part)]
    return (jnp.stack(outputs), cached_key_rows, cached_value_rows)


def solution(mesh):
    in_specs = (
        P(None, None, "blk"),
        P("blk"),
        P("blk", "kv"),
        P("kv", "blk"),
        P("blk"),
        P("blk", "kv"),
        P("blk", "kv"),
        P("kv", "blk"),
        P("blk", "kv", None, None),
        P("blk", "kv", None, None),
        P("blk", "kv", None, None),
        P("blk", "kv", None, None),
        P(None, "blk"),
        P(),
        P(),
        P("blk"),
    )
    out_specs = (P(None, None, "blk"), P("blk", "kv", None, None), P("blk", "kv", None, None))
    return jax.shard_map(body, mesh=mesh, in_specs=in_specs, out_specs=out_specs, check_vma=False)
```

profile of v0, /device:TPU:2, one launch (start us, length us, event | category | flops | bytes accessed | tf_op | source)
XLA Modules:
  0.0 210.3 jit_solution(3467085731439705462)
XLA Ops:
  0.7 1.0 copy.159
  1.7 0.8 fusion.23
  2.5 0.2 concatenate.90
  2.7 1.1 fusion.21
  3.9 0.9 pad_maximum_fusion.1
  4.8 7.6 %all-to-all-start = ((f32[32,8,641]{2,1,0:T(8,128)}), f32[32,8,641]{2,1,0:T(8,128)S(1)}, u32[]{:S(2)}, u32[]{:S(2)}) async-start(f32[32,8,641]{2,1,0:T(8,128)} %pad_maximum_fusion.1), calls=%async_computation | async-start | bytes 1572864 | tf_op jit(solution)/shard_map/all_to_all | solution.py:37
  13.3 0.6 gather_fusion
  13.9 0.6 gather_fusion.1
  14.6 1.0 compare_and_fusion
  15.5 0.9 bitcast_select_fusion.1
  16.4 9.3 %all-to-all-done = f32[32,8,641]{2,1,0:T(8,128)S(1)} async-done(((f32[32,8,641]{2,1,0:T(8,128)}), f32[32,8,641]{2,1,0:T(8,128)S(1)}, u32[]{:S(2)}, u32[]{:S(2)}) %all-to-all-start) | async-done | bytes 656416 | tf_op jit(solution)/shard_map/all_to_all | solution.py:37
  26.2 22.9 %all_gather.9 = bf16[256,1,3,128]{3,0,2,1:T(8,128)(2,1)S(1)} all-gather(bf16[8,1,3,128]{3,0,2,1:T(8,128)(2,1)S(1)} %pad_maximum_fusion.2), channel_id=1, replica_groups=mesh['kv'=8,'blk'=32] {'blk'}, dimensions={0}, use_global_device_ids=true | all-gather | bytes 202752 | tf_op jit(solution)/shard_map/all_gather | solution.py:126
  49.0 1.8 select_reduce_fusion
  50.9 3.1 %fusion.2 = (bf16[32,8,3,1024]{3,1,0,2:T(8,128)(2,1)}, f32[256,3]{0,1:T(4,128)S(1)}) fusion(f32[256,3,1024]{2,0,1:T(8,128)S(1)} %get-tuple-element.71, f32[256,3]{0,1:T(4,128)S(1)} %get-tuple-element.70, pred[256,1024]{1,0:T(8,128)(4,1)} %compare_and_fusion), kind=kLoop, calls=%fused_computation.8 | loop fusion | flops 3931392 | bytes 4986880 | tf_op jit(solution)/shard_map/reshape.462
  54.1 0.6 copy.163
  54.7 0.6 copy.162
  55.4 2.0 fusion.5
  57.4 1.1 maximum_bitcast_fusion
  58.5 5.7 %all-to-all-start.1 = ((f32[32,8,1,3,130]{4,1,3,2,0:T(8,128)}), f32[32,8,1,3,130]{4,1,3,2,0:T(8,128)S(1)}, u32[]{:S(2)}, u32[]{:S(2)}) async-start(f32[32,8,1,3,130]{4,1,3,2,0:T(8,128)} %maximum_bitcast_fusion), calls=%async_computation.1 | async-start | bytes 1572864 | tf_op jit(solution)/shard_map/all_to_all | solution.py:155
  64.6 0.3 select_reduce_fusion.1
  65.1 12.5 %all-to-all-done.1 = f32[32,8,1,3,130]{4,1,3,2,0:T(8,128)S(1)} async-done(((f32[32,8,1,3,130]{4,1,3,2,0:T(8,128)}), f32[32,8,1,3,130]{4,1,3,2,0:T(8,128)S(1)}, u32[]{:S(2)}, u32[]{:S(2)}) %all-to-all-start.1) | async-done | bytes 399392 | tf_op jit(solution)/shard_map/all_to_all | solution.py:155
  77.5 0.2 fusion.61
  77.7 0.2 copy.185
  78.0 0.2 copy.186
  78.3 0.2 fusion.32
  78.5 0.2 fusion.33
  79.0 0.2 fusion.12
  79.2 0.2 fusion.10
  79.5 23.1 %all_gather.10 = bf16[256,384]{1,0:T(8,128)(2,1)S(1)} all-gather(bf16[8,384]{1,0:T(8,128)(2,1)S(1)} %bitcast.108), channel_id=1, replica_groups=mesh['kv'=8,'blk'=32] {'blk'}, dimensions={0}, use_global_device_ids=true | all-gather | bytes 202752 | tf_op jit(solution)/shard_map/all_gather | solution.py:189
  102.6 0.2 fusion.62
  102.8 2.0 collective-permute-start
  104.8 3.3 %collective-permute-done = f32[256,96]{0,1:T(8,128)S(1)} collective-permute-done((f32[256,96]{0,1:T(8,128)S(1)}, f32[256,96]{0,1:T(8,128)S(1)}, u32[]{:S(2)}, u32[]{:S(2)}) %collective-permute-start) | collective-permute-done | bytes 98336 | tf_op jit(solution)/shard_map/ppermute | solution.py:22
  108.1 3.4 %collective-permute-start.1 = (f32[256,96]{0,1:T(8,128)S(1)}, f32[256,96]{0,1:T(8,128)S(1)}, u32[]{:S(2)}, u32[]{:S(2)}) collective-permute-start(f32[256,96]{0,1:T(8,128)S(1)} %add.109), channel_id=1, source_target_pairs={{0,64},{32,96},{64,0},{96,32},{128,192},{160,224},{192,128},{224,1... | collective-permute-start | bytes 294920 | tf_op jit(solution)/shard_map/ppermute | solution.py:22
  111.4 4.8 %collective-permute-done.1 = f32[256,96]{0,1:T(8,128)S(1)} collective-permute-done((f32[256,96]{0,1:T(8,128)S(1)}, f32[256,96]{0,1:T(8,128)S(1)}, u32[]{:S(2)}, u32[]{:S(2)}) %collective-permute-start.1) | collective-permute-done | bytes 98336 | tf_op jit(solution)/shard_map/ppermute | solution.py:22
  116.3 6.3 %collective-permute-start.2 = (f32[256,96]{0,1:T(8,128)S(1)}, f32[256,96]{0,1:T(8,128)S(1)}, u32[]{:S(2)}, u32[]{:S(2)}) collective-permute-start(f32[256,96]{0,1:T(8,128)S(1)} %add.110), channel_id=1, source_target_pairs={{0,128},{32,160},{64,192},{96,224},{128,0},{160,32},{192,64},{224,... | collective-permute-start | bytes 294920 | tf_op jit(solution)/shard_map/ppermute | solution.py:22
  122.5 3.6 %collective-permute-done.2 = f32[256,96]{0,1:T(8,128)S(1)} collective-permute-done((f32[256,96]{0,1:T(8,128)S(1)}, f32[256,96]{0,1:T(8,128)S(1)}, u32[]{:S(2)}, u32[]{:S(2)}) %collective-permute-start.2) | collective-permute-done | bytes 98336 | tf_op jit(solution)/shard_map/ppermute | solution.py:22
  126.2 0.2 concatenate.91
  126.5 0.5 convolution_bitcast_fusion
  127.0 0.2 pad_maximum_fusion
  127.2 34.6 %all_to_all.15 = f32[32,8,2049]{2,1,0:T(8,128)S(1)} all-to-all(f32[32,8,2049]{2,1,0:T(8,128)S(1)} %pad_maximum_fusion), channel_id=1, replica_groups=mesh['kv'=8,'blk'=32] {'blk'}, dimensions={0} | all-to-all | bytes 4196352 | tf_op jit(solution)/shard_map/all_to_all | solution.py:37
  162.1 23.3 %all_gather.11 = bf16[256,1024]{1,0:T(8,128)(2,1)S(1)} all-gather(bf16[8,1024]{1,0:T(8,128)(2,1)S(1)} %fusion.28), channel_id=1, replica_groups=mesh['kv'=8,'blk'=32] {'blk'}, dimensions={0}, use_global_device_ids=true | all-gather | bytes 540672 | tf_op jit(solution)/shard_map/all_gather | solution.py:208
  185.5 0.3 fusion.63
  185.9 5.0 %collective-permute-done.3 = f32[256,96]{0,1:T(8,128)S(1)} collective-permute-done((f32[256,96]{0,1:T(8,128)S(1)}, f32[256,96]{0,1:T(8,128)S(1)}, u32[]{:S(2)}, u32[]{:S(2)}) %collective-permute-start.3) | collective-permute-done | bytes 98336 | tf_op jit(solution)/shard_map/ppermute | solution.py:22
  190.9 3.3 %collective-permute-start.4 = (f32[256,96]{0,1:T(8,128)S(1)}, f32[256,96]{0,1:T(8,128)S(1)}, u32[]{:S(2)}, u32[]{:S(2)}) collective-permute-start(f32[256,96]{0,1:T(8,128)S(1)} %add.115), channel_id=1, source_target_pairs={{0,64},{32,96},{64,0},{96,32},{128,192},{160,224},{192,128},{224,1... | collective-permute-start | bytes 294920 | tf_op jit(solution)/shard_map/ppermute | solution.py:22
  194.2 4.8 %collective-permute-done.4 = f32[256,96]{0,1:T(8,128)S(1)} collective-permute-done((f32[256,96]{0,1:T(8,128)S(1)}, f32[256,96]{0,1:T(8,128)S(1)}, u32[]{:S(2)}, u32[]{:S(2)}) %collective-permute-start.4) | collective-permute-done | bytes 98336 | tf_op jit(solution)/shard_map/ppermute | solution.py:22
  199.0 4.3 %collective-permute-start.5 = (f32[256,96]{0,1:T(8,128)S(1)}, f32[256,96]{0,1:T(8,128)S(1)}, u32[]{:S(2)}, u32[]{:S(2)}) collective-permute-start(f32[256,96]{0,1:T(8,128)S(1)} %add.116), channel_id=1, source_target_pairs={{0,128},{32,160},{64,192},{96,224},{128,0},{160,32},{192,64},{224,... | collective-permute-start | bytes 294920 | tf_op jit(solution)/shard_map/ppermute | solution.py:22
  203.4 6.2 %collective-permute-done.5 = f32[256,96]{0,1:T(8,128)S(1)} collective-permute-done((f32[256,96]{0,1:T(8,128)S(1)}, f32[256,96]{0,1:T(8,128)S(1)}, u32[]{:S(2)}, u32[]{:S(2)}) %collective-permute-start.5) | collective-permute-done | bytes 98336 | tf_op jit(solution)/shard_map/ppermute | solution.py:22
  209.6 0.7 add_bitcast_fusion
  (87 shorter events, 2.9 us)
Async XLA Ops:
  0.6 48.4 %copy-start = (bf16[8,1,128,128]{3,2,1,0:T(8,128)(2,1)S(1)}, bf16[8,1,128,128]{3,2,1,0:T(8,128)(2,1)}, u32[]{:S(2)}) copy-start(bf16[8,1,128,128]{3,2,1,0:T(8,128)(2,1)} %param.30) | copy-start | bytes 786436
  0.6 11.8 %copy-start.12 = (s32[32]{0:T(128)S(1)}, s32[32]{0:T(128)}, u32[]{:S(2)}) copy-start(s32[32]{0:T(128)} %param.35) | copy-start | bytes 388
  0.7 12.0 %copy-start.14 = (s32[8]{0:T(128)S(1)}, s32[8]{0:T(128)}, u32[]{:S(2)}) copy-start(s32[8]{0:T(128)} %param.37) | copy-start | bytes 100
  0.7 12.0 %copy-start.15 = (s32[1,8]{1,0:T(1,128)S(1)}, s32[1,8]{1,0:T(1,128)}, u32[]{:S(2)}) copy-start(s32[1,8]{1,0:T(1,128)} %param.34) | copy-start | bytes 100
  0.7 12.1 %copy-start.6 = (bf16[8,1,127,128]{3,0,2,1:T(8,128)(2,1)S(1)}, bf16[8,1,127,128]{3,0,2,1:T(8,128)(2,1)}, u32[]{:S(2)}) copy-start(bf16[8,1,127,128]{3,0,2,1:T(8,128)(2,1)} %param.32) | copy-start | bytes 780292
  0.7 12.1 %copy-start.7 = (bf16[8,1,127,128]{3,0,2,1:T(8,128)(2,1)S(1)}, bf16[8,1,127,128]{3,0,2,1:T(8,128)(2,1)}, u32[]{:S(2)}) copy-start(bf16[8,1,127,128]{3,0,2,1:T(8,128)(2,1)} %param.33) | copy-start | bytes 780292
  2.7 10.5 %copy-start.16 = (s32[5]{0:T(128)S(1)}, s32[5]{0:T(128)}, u32[]{:S(2)}) copy-start(s32[5]{0:T(128)} %param.36) | copy-start | bytes 64
  4.8 20.9 %all-to-all-start = ((f32[32,8,641]{2,1,0:T(8,128)}), f32[32,8,641]{2,1,0:T(8,128)S(1)}, u32[]{:S(2)}, u32[]{:S(2)}) async-start(f32[32,8,641]{2,1,0:T(8,128)} %pad_maximum_fusion.1), calls=%async_computation | async-start | bytes 1572864 | tf_op jit(solution)/shard_map/all_to_all | solution.py:37
  54.7 9.7 %copy-start.1 = (bf16[8,1,128,128]{3,2,0,1:T(8,128)(2,1)S(1)}, bf16[8,1,128,128]{3,2,0,1:T(8,128)(2,1)}, u32[]{:S(2)}) copy-start(bf16[8,1,128,128]{3,2,0,1:T(8,128)(2,1)} %get-tuple-element.66) | copy-start | bytes 786436
  55.4 9.6 %copy-start.4 = (bf16[8,1,128,128]{3,2,0,1:T(8,128)(2,1)S(1)}, bf16[8,1,128,128]{3,2,0,1:T(8,128)(2,1)}, u32[]{:S(2)}) copy-start(bf16[8,1,128,128]{3,2,0,1:T(8,128)(2,1)} %get-tuple-element.67) | copy-start | bytes 786436
  58.5 44.1 %copy-start.11 = (bf16[384,96]{0,1:T(8,128)(2,1)S(1)}, bf16[384,96]{0,1:T(8,128)(2,1)}, u32[]{:S(2)}) copy-start(bf16[384,96]{0,1:T(8,128)(2,1)} %param.25) | copy-start | bytes 221188
  58.5 67.7 %copy-start.3 = (bf16[1,256,96]{1,2,0:T(8,128)(2,1)S(1)}, bf16[1,256,96]{1,2,0:T(8,128)(2,1)}, u32[]{:S(2)}) copy-start(bf16[1,256,96]{1,2,0:T(8,128)(2,1)} %param.22) | copy-start | bytes 147460
  58.5 68.0 %copy-start.8 = (bf16[96,1024]{1,0:T(8,128)(2,1)S(1)}, bf16[96,1024]{1,0:T(8,128)(2,1)}, u32[]{:S(2)}) copy-start(bf16[96,1024]{1,0:T(8,128)(2,1)} %param.28) | copy-start | bytes 589828
  58.5 68.0 %copy-start.9 = (bf16[96,1024]{1,0:T(8,128)(2,1)S(1)}, bf16[96,1024]{1,0:T(8,128)(2,1)}, u32[]{:S(2)}) copy-start(bf16[96,1024]{1,0:T(8,128)(2,1)} %param.27) | copy-start | bytes 589828
  58.5 68.0 %copy-start.13 = (f32[96]{0:T(128)S(1)}, f32[96]{0:T(128)}, u32[]{:S(2)}) copy-start(f32[96]{0:T(128)} %param.26) | copy-start | bytes 1156
  58.5 19.0 %all-to-all-start.1 = ((f32[32,8,1,3,130]{4,1,3,2,0:T(8,128)}), f32[32,8,1,3,130]{4,1,3,2,0:T(8,128)S(1)}, u32[]{:S(2)}, u32[]{:S(2)}) async-start(f32[32,8,1,3,130]{4,1,3,2,0:T(8,128)} %maximum_bitcast_fusion), calls=%async_computation.1 | async-start | bytes 1572864 | tf_op jit(solution)/shard_map/all_to_all | solution.py:155
  64.5 62.5 %copy-start.2 = (bf16[8,1,128,128]{3,2,0,1:T(8,128)(2,1)}, bf16[8,1,128,128]{3,2,0,1:T(8,128)(2,1)S(1)}, u32[]{:S(2)}) copy-start(bf16[8,1,128,128]{3,2,0,1:T(8,128)(2,1)S(1)} %scatter.6) | copy-start | bytes 786436
  65.0 62.0 %copy-start.5 = (bf16[8,1,128,128]{3,2,0,1:T(8,128)(2,1)}, bf16[8,1,128,128]{3,2,0,1:T(8,128)(2,1)S(1)}, u32[]{:S(2)}) copy-start(bf16[8,1,128,128]{3,2,0,1:T(8,128)(2,1)S(1)} %scatter.9) | copy-start | bytes 786436
  102.8 5.3 %collective-permute-start = (f32[256,96]{0,1:T(8,128)S(1)}, f32[256,96]{0,1:T(8,128)S(1)}, u32[]{:S(2)}, u32[]{:S(2)}) collective-permute-start(f32[256,96]{0,1:T(8,128)S(1)} %fusion.62), channel_id=1, source_target_pairs={{0,32},{32,0},{64,96},{96,64},{128,160},{160,128},{192,224},{224,1... | collective-permute-start | bytes 294920 | tf_op jit(solution)/shard_map/ppermute | solution.py:22
  108.1 8.2 %collective-permute-start.1 = (f32[256,96]{0,1:T(8,128)S(1)}, f32[256,96]{0,1:T(8,128)S(1)}, u32[]{:S(2)}, u32[]{:S(2)}) collective-permute-start(f32[256,96]{0,1:T(8,128)S(1)} %add.109), channel_id=1, source_target_pairs={{0,64},{32,96},{64,0},{96,32},{128,192},{160,224},{192,128},{224,1... | collective-permute-start | bytes 294920 | tf_op jit(solution)/shard_map/ppermute | solution.py:22
  116.3 9.9 %collective-permute-start.2 = (f32[256,96]{0,1:T(8,128)S(1)}, f32[256,96]{0,1:T(8,128)S(1)}, u32[]{:S(2)}, u32[]{:S(2)}) collective-permute-start(f32[256,96]{0,1:T(8,128)S(1)} %add.110), channel_id=1, source_target_pairs={{0,128},{32,160},{64,192},{96,224},{128,0},{160,32},{192,64},{224,... | collective-permute-start | bytes 294920 | tf_op jit(solution)/shard_map/ppermute | solution.py:22
  127.2 58.3 %copy-start.10 = (bf16[1024,96]{0,1:T(8,128)(2,1)S(1)}, bf16[1024,96]{0,1:T(8,128)(2,1)}, u32[]{:S(2)}) copy-start(bf16[1024,96]{0,1:T(8,128)(2,1)} %param.29) | copy-start | bytes 589828
  185.8 5.1 %collective-permute-start.3 = (f32[256,96]{0,1:T(8,128)S(1)}, f32[256,96]{0,1:T(8,128)S(1)}, u32[]{:S(2)}, u32[]{:S(2)}) collective-permute-start(f32[256,96]{0,1:T(8,128)S(1)} %fusion.63), channel_id=1, source_target_pairs={{0,32},{32,0},{64,96},{96,64},{128,160},{160,128},{192,224},{224,1... | collective-permute-start | bytes 294920 | tf_op jit(solution)/shard_map/ppermute | solution.py:22
  190.9 8.1 %collective-permute-start.4 = (f32[256,96]{0,1:T(8,128)S(1)}, f32[256,96]{0,1:T(8,128)S(1)}, u32[]{:S(2)}, u32[]{:S(2)}) collective-permute-start(f32[256,96]{0,1:T(8,128)S(1)} %add.115), channel_id=1, source_target_pairs={{0,64},{32,96},{64,0},{96,32},{128,192},{160,224},{192,128},{224,1... | collective-permute-start | bytes 294920 | tf_op jit(solution)/shard_map/ppermute | solution.py:22
  199.0 10.6 %collective-permute-start.5 = (f32[256,96]{0,1:T(8,128)S(1)}, f32[256,96]{0,1:T(8,128)S(1)}, u32[]{:S(2)}, u32[]{:S(2)}) collective-permute-start(f32[256,96]{0,1:T(8,128)S(1)} %add.116), channel_id=1, source_target_pairs={{0,128},{32,160},{64,192},{96,224},{128,0},{160,32},{192,64},{224,... | collective-permute-start | bytes 294920 | tf_op jit(solution)/shard_map/ppermute | solution.py:22
where the time goes:
time: 211 us; the launch traced here: 210 us
  blocking collectives  104 us (49%)
  waiting for transfers between devices  49.7 us (24%)
  starting transfers between devices  32.7 us (15%)
  other arithmetic  10.9 us (5%)
  matrix products  6.5 us (3%)
  local copies, waits for them, and re-layouts  5.57 us (3%)
    all_to_all x1, blocking collectives, scatter_sum(): return jnp.sum(lax.all_to_all(pieces, axis, 0, 0, tiled=False), axis=0)  34.6 us
    ppermute x6, waiting for transfers between devices, exchange(): return lax.ppermute(value, axis, [(i, i ^ 1 << bit) for i in range(count)])  27.9 us
    all_gather x1, blocking collectives, body(): lax.all_gather(hidden, 'blk', axis=0, tiled=True)  23.3 us
    all_gather x1, blocking collectives, body(): lax.all_gather(heads_out, 'blk', axis=0, tiled=True)  23.1 us
    all_gather x1, blocking collectives, body(): query_rows = lax.all_gather(own_queries, 'blk', axis=0, tiled=True)  22.9 us
    ppermute x6, starting transfers between devices, exchange(): return lax.ppermute(value, axis, [(i, i ^ 1 << bit) for i in range(count)])  19.3 us
    all_to_all x1, waiting for transfers between devices, body(): parts = lax.all_to_all(packed, 'blk', 0, 0, tiled=False)  12.5 us
    all_to_all x1, waiting for transfers between devices, scatter_sum(): return jnp.sum(lax.all_to_all(pieces, axis, 0, 0, tiled=False), axis=0)  9.32 us
  transfers between devices with their start and end apart: 8, of which 8 were waited for; matrix products, arithmetic and copies ran while one was open for 2% of the time, Pallas kernels for 0%

commit v1 on v0

--- a/solution.py
+++ b/solution.py
@@ -15,6 +15,11 @@
 EARLIER_TOKENS = 127
 DECODE_STEPS = 1
 masked_score = -1e30
+
+
+def tiled_gather(x, axis, dim):
+    copies = jnp.concatenate([x] * lax.axis_size(axis), axis=dim)
+    return lax.all_to_all(copies, axis, dim, dim, tiled=True)
 
 
 def exchange(value, axis, bit):
@@ -204,11 +209,7 @@
     gate = mixed[:, :unit_count] * own_inverse[:, None]
     upper = mixed[:, unit_count : 2 * unit_count] * own_inverse[:, None]
     hidden = (jax.nn.silu(gate) * upper).astype(jnp.bfloat16)
-    ff_part = jnp.dot(
-        lax.all_gather(hidden, "blk", axis=0, tiled=True),
-        w_down,
-        preferred_element_type=jnp.float32,
-    )
+    ff_part = jnp.dot(tiled_gather(hidden, "blk", 0), w_down, preferred_element_type=jnp.float32)
     outputs = [after_attn + across_heads(ff_part)]
     return (jnp.stack(outputs), cached_key_rows, cached_value_rows)
 

time: 211 us -> 203 us (0.962)
  blocking collectives: 104 us -> 95.6 us
    all_gather x1 -> x0, blocking collectives: 23.3 us -> none  [body(): lax.all_gather(hidden, 'blk', axis=0, tiled=True)]
    all_to_all x0 -> x1, blocking collectives: none -> 15.1 us  [tiled_gather(): return lax.all_to_all(copies, axis, dim, dim, tiled=True)]
where the time goes in v1:
time: 203 us; the launch traced here: 202 us
  blocking collectives  95.6 us (47%)
  waiting for transfers between devices  49.7 us (24%)
  starting transfers between devices  32.7 us (16%)
  other arithmetic  10.9 us (5%)
  matrix products  6.5 us (3%)
  local copies, waits for them, and re-layouts  5.68 us (3%)
    all_to_all x1, blocking collectives, scatter_sum(): return jnp.sum(lax.all_to_all(pieces, axis, 0, 0, tiled=False), axis=0)  34.5 us
    ppermute x6, waiting for transfers between devices, exchange(): return lax.ppermute(value, axis, [(i, i ^ 1 << bit) for i in range(count)])  27.9 us
    all_gather x1, blocking collectives, body(): lax.all_gather(heads_out, 'blk', axis=0, tiled=True)  23.1 us
    all_gather x1, blocking collectives, body(): query_rows = lax.all_gather(own_queries, 'blk', axis=0, tiled=True)  22.9 us
    ppermute x6, starting transfers between devices, exchange(): return lax.ppermute(value, axis, [(i, i ^ 1 << bit) for i in range(count)])  19.3 us
    all_to_all x1, blocking collectives, tiled_gather(): return lax.all_to_all(copies, axis, dim, dim, tiled=True)  15.1 us
    all_to_all x1, waiting for transfers between devices, body(): parts = lax.all_to_all(packed, 'blk', 0, 0, tiled=False)  12.5 us
    all_to_all x1, waiting for transfers between devices, scatter_sum(): return jnp.sum(lax.all_to_all(pieces, axis, 0, 0, tiled=False), axis=0)  9.32 us
  transfers between devices with their start and end apart: 8, of which 8 were waited for; matrix products, arithmetic and copies ran while one was open for 2% of the time, Pallas kernels for 0%

profile of v1, /device:TPU:2, one launch (start us, length us, event | category | flops | bytes accessed | tf_op | source)
XLA Modules:
  0.0 202.4 jit_solution(18270273555033511758)
XLA Ops:
  0.7 1.0 copy.159
  1.7 0.8 fusion.25
  2.5 0.2 concatenate.94
  2.7 1.1 fusion.23
  3.9 0.9 pad_maximum_fusion.1
  4.8 7.6 %all-to-all-start = ((f32[32,8,641]{2,1,0:T(8,128)}), f32[32,8,641]{2,1,0:T(8,128)S(1)}, u32[]{:S(2)}, u32[]{:S(2)}) async-start(f32[32,8,641]{2,1,0:T(8,128)} %pad_maximum_fusion.1), calls=%async_computation | async-start | bytes 1572864 | tf_op jit(solution)/shard_map/all_to_all | solution.py:42
  13.3 0.6 gather_fusion
  13.9 0.6 gather_fusion.1
  14.6 1.0 compare_and_fusion
  15.5 0.9 bitcast_select_fusion.1
  16.4 9.3 %all-to-all-done = f32[32,8,641]{2,1,0:T(8,128)S(1)} async-done(((f32[32,8,641]{2,1,0:T(8,128)}), f32[32,8,641]{2,1,0:T(8,128)S(1)}, u32[]{:S(2)}, u32[]{:S(2)}) %all-to-all-start) | async-done | bytes 656416 | tf_op jit(solution)/shard_map/all_to_all | solution.py:42
  26.2 22.9 %all_gather.6 = bf16[256,1,3,128]{3,0,2,1:T(8,128)(2,1)S(1)} all-gather(bf16[8,1,3,128]{3,0,2,1:T(8,128)(2,1)S(1)} %pad_maximum_fusion.2), channel_id=1, replica_groups=mesh['kv'=8,'blk'=32] {'blk'}, dimensions={0}, use_global_device_ids=true | all-gather | bytes 202752 | tf_op jit(solution)/shard_map/all_gather | solution.py:131
  49.0 1.8 select_reduce_fusion
  50.9 3.1 %fusion.2 = (bf16[32,8,3,1024]{3,1,0,2:T(8,128)(2,1)}, f32[256,3]{0,1:T(4,128)S(1)}) fusion(f32[256,3,1024]{2,0,1:T(8,128)S(1)} %get-tuple-element.73, f32[256,3]{0,1:T(4,128)S(1)} %get-tuple-element.72, pred[256,1024]{1,0:T(8,128)(4,1)} %compare_and_fusion), kind=kLoop, calls=%fused_computation.8 | loop fusion | flops 3931392 | bytes 4986880 | tf_op jit(solution)/shard_map/reshape.464
  54.1 0.6 copy.163
  54.7 0.6 copy.162
  55.4 2.0 %fusion.5 = f32[32,8,1,3,128]{4,1,3,0,2:T(8,128)S(1)} fusion(bf16[1024,128,1,1]{1,0,3,2:T(8,128)(2,1)} %bitcast.113, bf16[32,8,3,1024]{3,1,0,2:T(8,128)(2,1)} %get-tuple-element.57), kind=kOutput, calls=%fused_computation.11 | convolution fusion | flops 201326592 | bytes 2228224 | tf_op jit(solution)/shard_map/kqn,knd->kqd/dot_general | solution.py:152
  57.4 1.1 maximum_bitcast_fusion
  58.5 5.7 %all-to-all-start.1 = ((f32[32,8,1,3,130]{4,1,3,2,0:T(8,128)}), f32[32,8,1,3,130]{4,1,3,2,0:T(8,128)S(1)}, u32[]{:S(2)}, u32[]{:S(2)}) async-start(f32[32,8,1,3,130]{4,1,3,2,0:T(8,128)} %maximum_bitcast_fusion), calls=%async_computation.1 | async-start | bytes 1572864 | tf_op jit(solution)/shard_map/all_to_all | solution.py:160
  64.6 0.3 select_reduce_fusion.1
  65.0 12.5 %all-to-all-done.1 = f32[32,8,1,3,130]{4,1,3,2,0:T(8,128)S(1)} async-done(((f32[32,8,1,3,130]{4,1,3,2,0:T(8,128)}), f32[32,8,1,3,130]{4,1,3,2,0:T(8,128)S(1)}, u32[]{:S(2)}, u32[]{:S(2)}) %all-to-all-start.1) | async-done | bytes 399392 | tf_op jit(solution)/shard_map/all_to_all | solution.py:160
  77.5 0.2 fusion.64
  77.7 0.2 copy.185
  77.9 0.2 copy.186
  78.2 0.2 fusion.34
  78.5 0.2 fusion.35
  79.0 0.2 fusion.14
  79.2 0.2 fusion.10
  79.5 23.1 %all_gather.7 = bf16[256,384]{1,0:T(8,128)(2,1)S(1)} all-gather(bf16[8,384]{1,0:T(8,128)(2,1)S(1)} %bitcast.112), channel_id=1, replica_groups=mesh['kv'=8,'blk'=32] {'blk'}, dimensions={0}, use_global_device_ids=true | all-gather | bytes 202752 | tf_op jit(solution)/shard_map/all_gather | solution.py:194
  102.6 0.2 fusion.65
  102.8 2.0 collective-permute-start
  104.8 3.3 %collective-permute-done = f32[256,96]{0,1:T(8,128)S(1)} collective-permute-done((f32[256,96]{0,1:T(8,128)S(1)}, f32[256,96]{0,1:T(8,128)S(1)}, u32[]{:S(2)}, u32[]{:S(2)}) %collective-permute-start) | collective-permute-done | bytes 98336 | tf_op jit(solution)/shard_map/ppermute | solution.py:27
  108.1 3.3 %collective-permute-start.1 = (f32[256,96]{0,1:T(8,128)S(1)}, f32[256,96]{0,1:T(8,128)S(1)}, u32[]{:S(2)}, u32[]{:S(2)}) collective-permute-start(f32[256,96]{0,1:T(8,128)S(1)} %add.109), channel_id=1, source_target_pairs={{0,64},{32,96},{64,0},{96,32},{128,192},{160,224},{192,128},{224,1... | collective-permute-start | bytes 294920 | tf_op jit(solution)/shard_map/ppermute | solution.py:27
  111.4 4.8 %collective-permute-done.1 = f32[256,96]{0,1:T(8,128)S(1)} collective-permute-done((f32[256,96]{0,1:T(8,128)S(1)}, f32[256,96]{0,1:T(8,128)S(1)}, u32[]{:S(2)}, u32[]{:S(2)}) %collective-permute-start.1) | collective-permute-done | bytes 98336 | tf_op jit(solution)/shard_map/ppermute | solution.py:27
  116.3 6.3 %collective-permute-start.2 = (f32[256,96]{0,1:T(8,128)S(1)}, f32[256,96]{0,1:T(8,128)S(1)}, u32[]{:S(2)}, u32[]{:S(2)}) collective-permute-start(f32[256,96]{0,1:T(8,128)S(1)} %add.110), channel_id=1, source_target_pairs={{0,128},{32,160},{64,192},{96,224},{128,0},{160,32},{192,64},{224,... | collective-permute-start | bytes 294920 | tf_op jit(solution)/shard_map/ppermute | solution.py:27
  122.5 3.6 %collective-permute-done.2 = f32[256,96]{0,1:T(8,128)S(1)} collective-permute-done((f32[256,96]{0,1:T(8,128)S(1)}, f32[256,96]{0,1:T(8,128)S(1)}, u32[]{:S(2)}, u32[]{:S(2)}) %collective-permute-start.2) | collective-permute-done | bytes 98336 | tf_op jit(solution)/shard_map/ppermute | solution.py:27
  126.2 0.2 concatenate.95
  126.5 0.5 convolution_bitcast_fusion
  127.0 0.2 pad_maximum_fusion
  127.2 34.5 %all_to_all.27 = f32[32,8,2049]{2,1,0:T(8,128)S(1)} all-to-all(f32[32,8,2049]{2,1,0:T(8,128)S(1)} %pad_maximum_fusion), channel_id=1, replica_groups=mesh['kv'=8,'blk'=32] {'blk'}, dimensions={0} | all-to-all | bytes 4196352 | tf_op jit(solution)/shard_map/all_to_all | solution.py:42
  162.3 15.1 %all_to_all.28 = bf16[32,8,1024]{2,1,0:T(8,128)(2,1)S(1)} all-to-all(bf16[32,8,1024]{2,1,0:T(8,128)(2,1)S(1)} %bitcast.108), channel_id=1, replica_groups=mesh['kv'=8,'blk'=32] {'blk'}, dimensions={0} | all-to-all | bytes 1048576 | tf_op jit(solution)/shard_map/all_to_all | solution.py:22
  177.5 0.3 fusion.11
  177.9 5.0 %collective-permute-done.3 = f32[256,96]{0,1:T(8,128)S(1)} collective-permute-done((f32[256,96]{0,1:T(8,128)S(1)}, f32[256,96]{0,1:T(8,128)S(1)}, u32[]{:S(2)}, u32[]{:S(2)}) %collective-permute-start.3) | collective-permute-done | bytes 98336 | tf_op jit(solution)/shard_map/ppermute | solution.py:27
  183.0 3.2 %collective-permute-start.4 = (f32[256,96]{0,1:T(8,128)S(1)}, f32[256,96]{0,1:T(8,128)S(1)}, u32[]{:S(2)}, u32[]{:S(2)}) collective-permute-start(f32[256,96]{0,1:T(8,128)S(1)} %add.115), channel_id=1, source_target_pairs={{0,64},{32,96},{64,0},{96,32},{128,192},{160,224},{192,128},{224,1... | collective-permute-start | bytes 294920 | tf_op jit(solution)/shard_map/ppermute | solution.py:27
  186.2 4.8 %collective-permute-done.4 = f32[256,96]{0,1:T(8,128)S(1)} collective-permute-done((f32[256,96]{0,1:T(8,128)S(1)}, f32[256,96]{0,1:T(8,128)S(1)}, u32[]{:S(2)}, u32[]{:S(2)}) %collective-permute-start.4) | collective-permute-done | bytes 98336 | tf_op jit(solution)/shard_map/ppermute | solution.py:27
  191.1 4.4 %collective-permute-start.5 = (f32[256,96]{0,1:T(8,128)S(1)}, f32[256,96]{0,1:T(8,128)S(1)}, u32[]{:S(2)}, u32[]{:S(2)}) collective-permute-start(f32[256,96]{0,1:T(8,128)S(1)} %add.116), channel_id=1, source_target_pairs={{0,128},{32,160},{64,192},{96,224},{128,0},{160,32},{192,64},{224,... | collective-permute-start | bytes 294920 | tf_op jit(solution)/shard_map/ppermute | solution.py:27
  195.4 6.3 %collective-permute-done.5 = f32[256,96]{0,1:T(8,128)S(1)} collective-permute-done((f32[256,96]{0,1:T(8,128)S(1)}, f32[256,96]{0,1:T(8,128)S(1)}, u32[]{:S(2)}, u32[]{:S(2)}) %collective-permute-start.5) | collective-permute-done | bytes 98336 | tf_op jit(solution)/shard_map/ppermute | solution.py:27
  201.7 0.7 add_bitcast_fusion
  (118 shorter events, 3.0 us)
Async XLA Ops:
  0.6 48.4 %copy-start = (bf16[8,1,128,128]{3,2,1,0:T(8,128)(2,1)S(1)}, bf16[8,1,128,128]{3,2,1,0:T(8,128)(2,1)}, u32[]{:S(2)}) copy-start(bf16[8,1,128,128]{3,2,1,0:T(8,128)(2,1)} %param.30) | copy-start | bytes 786436
  0.6 11.8 %copy-start.12 = (s32[32]{0:T(128)S(1)}, s32[32]{0:T(128)}, u32[]{:S(2)}) copy-start(s32[32]{0:T(128)} %param.35) | copy-start | bytes 388
  0.7 12.0 %copy-start.14 = (s32[8]{0:T(128)S(1)}, s32[8]{0:T(128)}, u32[]{:S(2)}) copy-start(s32[8]{0:T(128)} %param.37) | copy-start | bytes 100
  0.7 12.0 %copy-start.15 = (s32[1,8]{1,0:T(1,128)S(1)}, s32[1,8]{1,0:T(1,128)}, u32[]{:S(2)}) copy-start(s32[1,8]{1,0:T(1,128)} %param.34) | copy-start | bytes 100
  0.7 12.1 %copy-start.6 = (bf16[8,1,127,128]{3,0,2,1:T(8,128)(2,1)S(1)}, bf16[8,1,127,128]{3,0,2,1:T(8,128)(2,1)}, u32[]{:S(2)}) copy-start(bf16[8,1,127,128]{3,0,2,1:T(8,128)(2,1)} %param.32) | copy-start | bytes 780292
  0.7 12.1 %copy-start.7 = (bf16[8,1,127,128]{3,0,2,1:T(8,128)(2,1)S(1)}, bf16[8,1,127,128]{3,0,2,1:T(8,128)(2,1)}, u32[]{:S(2)}) copy-start(bf16[8,1,127,128]{3,0,2,1:T(8,128)(2,1)} %param.33) | copy-start | bytes 780292
  2.7 10.4 %copy-start.16 = (s32[5]{0:T(128)S(1)}, s32[5]{0:T(128)}, u32[]{:S(2)}) copy-start(s32[5]{0:T(128)} %param.36) | copy-start | bytes 64
  4.8 20.9 %all-to-all-start = ((f32[32,8,641]{2,1,0:T(8,128)}), f32[32,8,641]{2,1,0:T(8,128)S(1)}, u32[]{:S(2)}, u32[]{:S(2)}) async-start(f32[32,8,641]{2,1,0:T(8,128)} %pad_maximum_fusion.1), calls=%async_computation | async-start | bytes 1572864 | tf_op jit(solution)/shard_map/all_to_all | solution.py:42
  54.7 9.7 %copy-start.1 = (bf16[8,1,128,128]{3,2,0,1:T(8,128)(2,1)S(1)}, bf16[8,1,128,128]{3,2,0,1:T(8,128)(2,1)}, u32[]{:S(2)}) copy-start(bf16[8,1,128,128]{3,2,0,1:T(8,128)(2,1)} %get-tuple-element.68) | copy-start | bytes 786436
  55.4 9.6 %copy-start.4 = (bf16[8,1,128,128]{3,2,0,1:T(8,128)(2,1)S(1)}, bf16[8,1,128,128]{3,2,0,1:T(8,128)(2,1)}, u32[]{:S(2)}) copy-start(bf16[8,1,128,128]{3,2,0,1:T(8,128)(2,1)} %get-tuple-element.69) | copy-start | bytes 786436
  58.5 44.1 %copy-start.11 = (bf16[384,96]{0,1:T(8,128)(2,1)S(1)}, bf16[384,96]{0,1:T(8,128)(2,1)}, u32[]{:S(2)}) copy-start(bf16[384,96]{0,1:T(8,128)(2,1)} %param.25) | copy-start | bytes 221188
  58.5 67.7 %copy-start.3 = (bf16[1,256,96]{1,2,0:T(8,128)(2,1)S(1)}, bf16[1,256,96]{1,2,0:T(8,128)(2,1)}, u32[]{:S(2)}) copy-start(bf16[1,256,96]{1,2,0:T(8,128)(2,1)} %param.22) | copy-start | bytes 147460
  58.5 68.0 %copy-start.8 = (bf16[96,1024]{1,0:T(8,128)(2,1)S(1)}, bf16[96,1024]{1,0:T(8,128)(2,1)}, u32[]{:S(2)}) copy-start(bf16[96,1024]{1,0:T(8,128)(2,1)} %param.28) | copy-start | bytes 589828
  58.5 68.0 %copy-start.9 = (bf16[96,1024]{1,0:T(8,128)(2,1)S(1)}, bf16[96,1024]{1,0:T(8,128)(2,1)}, u32[]{:S(2)}) copy-start(bf16[96,1024]{1,0:T(8,128)(2,1)} %param.27) | copy-start | bytes 589828
  58.5 68.0 %copy-start.13 = (f32[96]{0:T(128)S(1)}, f32[96]{0:T(128)}, u32[]{:S(2)}) copy-start(f32[96]{0:T(128)} %param.26) | copy-start | bytes 1156
  58.5 19.0 %all-to-all-start.1 = ((f32[32,8,1,3,130]{4,1,3,2,0:T(8,128)}), f32[32,8,1,3,130]{4,1,3,2,0:T(8,128)S(1)}, u32[]{:S(2)}, u32[]{:S(2)}) async-start(f32[32,8,1,3,130]{4,1,3,2,0:T(8,128)} %maximum_bitcast_fusion), calls=%async_computation.1 | async-start | bytes 1572864 | tf_op jit(solution)/shard_map/all_to_all | solution.py:160
  64.5 62.5 %copy-start.2 = (bf16[8,1,128,128]{3,2,0,1:T(8,128)(2,1)}, bf16[8,1,128,128]{3,2,0,1:T(8,128)(2,1)S(1)}, u32[]{:S(2)}) copy-start(bf16[8,1,128,128]{3,2,0,1:T(8,128)(2,1)S(1)} %scatter.6) | copy-start | bytes 786436
  65.0 62.0 %copy-start.5 = (bf16[8,1,128,128]{3,2,0,1:T(8,128)(2,1)}, bf16[8,1,128,128]{3,2,0,1:T(8,128)(2,1)S(1)}, u32[]{:S(2)}) copy-start(bf16[8,1,128,128]{3,2,0,1:T(8,128)(2,1)S(1)} %scatter.9) | copy-start | bytes 786436
  102.8 5.3 %collective-permute-start = (f32[256,96]{0,1:T(8,128)S(1)}, f32[256,96]{0,1:T(8,128)S(1)}, u32[]{:S(2)}, u32[]{:S(2)}) collective-permute-start(f32[256,96]{0,1:T(8,128)S(1)} %fusion.65), channel_id=1, source_target_pairs={{0,32},{32,0},{64,96},{96,64},{128,160},{160,128},{192,224},{224,1... | collective-permute-start | bytes 294920 | tf_op jit(solution)/shard_map/ppermute | solution.py:27
  108.1 8.1 %collective-permute-start.1 = (f32[256,96]{0,1:T(8,128)S(1)}, f32[256,96]{0,1:T(8,128)S(1)}, u32[]{:S(2)}, u32[]{:S(2)}) collective-permute-start(f32[256,96]{0,1:T(8,128)S(1)} %add.109), channel_id=1, source_target_pairs={{0,64},{32,96},{64,0},{96,32},{128,192},{160,224},{192,128},{224,1... | collective-permute-start | bytes 294920 | tf_op jit(solution)/shard_map/ppermute | solution.py:27
  116.3 9.9 %collective-permute-start.2 = (f32[256,96]{0,1:T(8,128)S(1)}, f32[256,96]{0,1:T(8,128)S(1)}, u32[]{:S(2)}, u32[]{:S(2)}) collective-permute-start(f32[256,96]{0,1:T(8,128)S(1)} %add.110), channel_id=1, source_target_pairs={{0,128},{32,160},{64,192},{96,224},{128,0},{160,32},{192,64},{224,... | collective-permute-start | bytes 294920 | tf_op jit(solution)/shard_map/ppermute | solution.py:27
  161.6 15.8 %copy-start.10 = (bf16[1024,96]{0,1:T(8,128)(2,1)S(1)}, bf16[1024,96]{0,1:T(8,128)(2,1)}, u32[]{:S(2)}) copy-start(bf16[1024,96]{0,1:T(8,128)(2,1)} %param.29) | copy-start | bytes 589828
  177.8 5.2 %collective-permute-start.3 = (f32[256,96]{0,1:T(8,128)S(1)}, f32[256,96]{0,1:T(8,128)S(1)}, u32[]{:S(2)}, u32[]{:S(2)}) collective-permute-start(f32[256,96]{0,1:T(8,128)S(1)} %fusion.11), channel_id=1, source_target_pairs={{0,32},{32,0},{64,96},{96,64},{128,160},{160,128},{192,224},{224,1... | collective-permute-start | bytes 294920 | tf_op jit(solution)/shard_map/ppermute | solution.py:27
  183.0 8.1 %collective-permute-start.4 = (f32[256,96]{0,1:T(8,128)S(1)}, f32[256,96]{0,1:T(8,128)S(1)}, u32[]{:S(2)}, u32[]{:S(2)}) collective-permute-start(f32[256,96]{0,1:T(8,128)S(1)} %add.115), channel_id=1, source_target_pairs={{0,64},{32,96},{64,0},{96,32},{128,192},{160,224},{192,128},{224,1... | collective-permute-start | bytes 294920 | tf_op jit(solution)/shard_map/ppermute | solution.py:27
  191.1 10.6 %collective-permute-start.5 = (f32[256,96]{0,1:T(8,128)S(1)}, f32[256,96]{0,1:T(8,128)S(1)}, u32[]{:S(2)}, u32[]{:S(2)}) collective-permute-start(f32[256,96]{0,1:T(8,128)S(1)} %add.116), channel_id=1, source_target_pairs={{0,128},{32,160},{64,192},{96,224},{128,0},{160,32},{192,64},{224,... | collective-permute-start | bytes 294920 | tf_op jit(solution)/shard_map/ppermute | solution.py:27
